TPU v7x, 256 devices: a whole 4x4x8 slice. The times are simulated.
256 devices in a mesh: seq: 16 (over y, x), fsdp: 16 (over z, core).
Axes of the slice: x: 4, y: 4, z: 8, core: 2. Of those that a mesh axis runs over, the one named last changes fastest.
Arguments:
- byte_rows: bfloat16 [16, 16384, 512], P('fsdp', 'seq'), may hold values from -6 to 6
- cotangent: bfloat16 [16, 16384, 512], P('fsdp', 'seq'), may hold values from -6 to 6
- doc_ids: int32 [16, 16384], P('fsdp', 'seq'), may hold values from 0 to 31, never falling along the last dimension, each value on 1 to 2048 neighbouring positions
- conv_weight: bfloat16 [8, 32, 16, 16], replicated, may hold values from -0.5 to 0.5
- norm_gain: float32 [512], replicated, may hold values from 0.5 to 1.5
- proj_weight: bfloat16 [4096, 512], P('fsdp'), may hold values from -0.25 to 0.25
- round_seed: int32 [1], replicated, may hold values from 0 to 1073741823
- step_count: int32 [1], replicated, may hold values from 0 to 999999
Outputs:
- grad_bytes: float32 [16, 16384, 512], P('fsdp', 'seq')
- grad_proj: float32 [4096, 512], P('fsdp')
- grad_conv: float32 [8, 32, 16, 16], replicated
- grad_gain: float32 [512], replicated
Inputs may be any that keep to these rules, and one draw needn't show every extreme that they name: `doc_ids`: along each sequence the document numbers never fall; no document covers more than 2048 bytes, and one covers exactly 2048.
All inputs are finite; a program needn't handle non-finite values.
Results may differ from a plain program's by a relative error of at most 0.0046.
Values may be sent and summed in bfloat16 or wider, within the bound.
No kernel may reach another device: no remote copies, remote signals or barrier semaphores. Data moves between devices by JAX's collectives and lax.ppermute only.
A program may use at most 128 MiB of HBM per device.

v0:
```python
import math
import jax
import jax.numpy as jnp
from jax import lax
from jax.sharding import PartitionSpec as P

GROUPS = 32
KERNEL = 8
STRIDE = 4
CG = 16
GELU_A = 0.7978845608028654
GELU_B = 0.044715
QUANT = 0.25


def shifted(value, axis, steps):
    count = lax.axis_size(axis)
    initial, last = (max(0, -steps), min(count, count - steps))
    return lax.ppermute(value, axis, [(source, source + steps) for source in range(initial, last)])


def gelu_grad(values):
    tangent = jnp.tanh(GELU_A * (values + GELU_B * values * values * values))
    return 0.5 * (1.0 + tangent) + 0.5 * values * (1.0 - tangent * tangent) * GELU_A * (
        1.0 + 3.0 * GELU_B * values * values
    )


def mix_bits(flat_index, seed_value, step_value):
    hashed = (
        flat_index * jnp.int32(-1640531535)
        + seed_value * jnp.int32(-2048144777)
        + step_value * jnp.int32(-1028477379)
    )
    hashed = hashed ^ lax.shift_right_logical(hashed, jnp.int32(16))
    hashed = hashed * jnp.int32(2146121005)
    hashed = hashed ^ lax.shift_right_logical(hashed, jnp.int32(15))
    hashed = hashed * jnp.int32(-2073254261)
    hashed = hashed ^ lax.shift_right_logical(hashed, jnp.int32(16))
    return lax.shift_right_logical(hashed, jnp.int32(8)).astype(jnp.float32) / 16777216.0


def tap_windows(series, extra_rows, patches):
    joined = jnp.concatenate([series, extra_rows], 0)
    tail_shape = joined.shape[1:]
    lower = joined[:-STRIDE].reshape((patches, STRIDE) + tail_shape)
    upper = joined[STRIDE:].reshape((patches, STRIDE) + tail_shape)
    return jnp.concatenate([lower, upper], 1)


def per_device(
    byte_rows, cotangent, doc_ids, conv_weight, norm_gain, proj_weight, round_seed, step_count
):
    byte_block = byte_rows[0]
    upstream = cotangent[0]
    doc_block = doc_ids[0]
    length = byte_block.shape[0]
    row_width = byte_block.shape[1]
    patches = length // STRIDE
    panel_rows = proj_weight.shape[0]
    full_width = panel_rows * lax.axis_size("fsdp")
    next_bytes, next_up, next_docs = shifted(
        (byte_block[:STRIDE], upstream[:STRIDE], doc_block[:STRIDE]), "seq", -1
    )
    window = tap_windows(byte_block, next_bytes, patches)
    up_window = tap_windows(upstream, next_up, patches)
    doc_window = tap_windows(doc_block, next_docs, patches)
    is_last = lax.axis_index("seq") == lax.axis_size("seq") - 1
    patch_ids = lax.broadcasted_iota(jnp.int32, (patches, KERNEL), 0)
    tap_ids = lax.broadcasted_iota(jnp.int32, (patches, KERNEL), 1)
    spilled = is_last & (patch_ids == patches - 1) & (tap_ids >= STRIDE)
    keep_tap = (doc_window == doc_window[:, :1]) & jnp.logical_not(spilled)
    keep_f = keep_tap.astype(jnp.float32)[:, :, None]
    masked = window * keep_tap.astype(jnp.bfloat16)[:, :, None]
    grouped = masked.reshape(patches, KERNEL, GROUPS, CG)
    hidden = jnp.einsum(
        "pkgc,kgcd->pgd", grouped, conv_weight, preferred_element_type=jnp.float32
    ).reshape(patches, row_width)
    factor = lax.rsqrt(jnp.mean(hidden * hidden, axis=-1, keepdims=True) + 1e-06)
    normed = (hidden * factor * norm_gain).astype(jnp.bfloat16)
    contract_last = (((1,), (1,)), ((), ()))
    full_proj = lax.all_gather(proj_weight, "fsdp", axis=0, tiled=True)
    pre_act = lax.dot_general(normed, full_proj, contract_last, preferred_element_type=jnp.float32)
    grad_pre = (
        up_window.astype(jnp.float32)
        * keep_f
        * gelu_grad(pre_act.reshape(patches, KERNEL, row_width))
    )
    grad_pre = grad_pre.reshape(patches, full_width).astype(jnp.bfloat16)
    grad_norm = jnp.dot(grad_pre, full_proj, preferred_element_type=jnp.float32)
    contract_first = (((0,), (0,)), ((), ()))
    panel_part = lax.psum_scatter(
        lax.dot_general(grad_pre, normed, contract_first, preferred_element_type=jnp.float32),
        "fsdp",
        scatter_dimension=0,
        tiled=True,
    )
    proj_sum = lax.psum(panel_part, "seq")
    gain_part = jnp.sum(grad_norm * hidden * factor, axis=0)
    gained = norm_gain * grad_norm
    grad_hidden = factor * gained - hidden * factor * factor * factor * jnp.mean(
        gained * hidden, axis=-1, keepdims=True
    )
    grad_hidden = grad_hidden.reshape(patches, GROUPS, CG)
    grouped_f = grouped.astype(jnp.float32)
    conv_f = conv_weight.astype(jnp.float32)
    conv_part = jnp.einsum(
        "pkgc,pgd->kgcd", grouped_f, grad_hidden, precision=lax.Precision.HIGHEST
    )
    gain_sum, conv_sum = lax.psum((gain_part, conv_part), ("seq", "fsdp"))
    grad_window = jnp.einsum("pgd,kgcd->pkgc", grad_hidden, conv_f, precision=lax.Precision.HIGHEST)
    grad_window = grad_window.reshape(patches, KERNEL, row_width) * keep_f
    back_lower = grad_window[:, :STRIDE].reshape(length, row_width)
    back_upper = grad_window[:, STRIDE:].reshape(length, row_width)
    incoming = shifted(back_upper[length - STRIDE :], "seq", 1)
    back_rows = back_lower + jnp.concatenate([incoming, back_upper[: length - STRIDE]], 0)
    grad_bytes = (upstream.astype(jnp.float32) + back_rows)[None]
    total_patches = patches * lax.axis_size("seq") * lax.axis_size("fsdp")
    grad_scale = 1.0 / math.sqrt(total_patches)
    first_panel = lax.axis_index("fsdp") * jnp.int32(panel_rows)
    row_index = first_panel + jnp.arange(panel_rows, dtype=jnp.int32)
    flat_index = (
        row_index[:, None] * jnp.int32(row_width) + jnp.arange(row_width, dtype=jnp.int32)[None, :]
    )
    dither_noise = mix_bits(flat_index, round_seed[0], step_count[0])
    grad_proj = proj_sum * grad_scale + QUANT * (dither_noise - 0.5)
    return (grad_bytes, grad_proj, conv_sum * grad_scale, gain_sum * grad_scale)


def solution(mesh):
    in_specs = (
        P("fsdp", "seq", None),
        P("fsdp", "seq", None),
        P("fsdp", "seq"),
        P(),
        P(),
        P("fsdp", None),
        P(),
        P(),
    )
    out_specs = (P("fsdp", "seq", None), P("fsdp", None), P(), P())
    return jax.shard_map(
        per_device, mesh=mesh, in_specs=in_specs, out_specs=out_specs, check_vma=False
    )
```

profile of v0, /device:TPU:32, one launch (start us, length us, event | category | flops | bytes accessed | tf_op | source)
XLA Modules:
  0.0 572.1 jit_solution(2157465076530851833)
XLA Ops:
  13.9 9.7 %concatenate.46 = bf16[256,4,32,16]{3,2,1,0:T(8,128)(2,1)} reshape(bf16[1,1024,512]{2,1,0:T(8,128)(2,1)} %param.8) | data formatting | bytes 2097152 | tf_op jit(solution)/shard_map/concatenate | solution.py:48
  25.2 9.8 %copy.43 = bf16[256,4,32,16]{0,3,2,1:T(8,128)(2,1)} copy(bf16[256,4,32,16]{3,2,1,0:T(8,128)(2,1)} %concatenate.46) | data formatting | bytes 2097152 | tf_op jit(solution)/shard_map/concatenate | solution.py:48
  35.0 3.1 copy.65
  40.2 8.2 %concatenate.48 = bf16[256,4,32,16]{3,2,1,0:T(8,128)(2,1)} reshape(bf16[1024,512]{1,0:T(8,128)(2,1)S(1)} %pad_maximum_fusion.1) | data formatting | bytes 2097152 | tf_op jit(solution)/shard_map/concatenate | solution.py:48
  48.4 9.8 %copy.44 = bf16[256,4,32,16]{0,3,2,1:T(8,128)(2,1)} copy(bf16[256,4,32,16]{3,2,1,0:T(8,128)(2,1)} %concatenate.48) | data formatting | bytes 2097152 | tf_op jit(solution)/shard_map/concatenate | solution.py:48
  63.6 7.9 %fusion.6 = bf16[256,8,512]{2,0,1:T(8,128)(2,1)} fusion(bf16[256,512,1]{0,1,2:T(8,128)(2,1)S(1)} %bitcast.62, bf16[8,512,512]{2,1,0:T(8,128)(2,1)} %bitcast.67, bf16[256,4,512]{2,0,1:T(8,128)(2,1)} %copy.50, bf16[256,4,512]{2,0,1:T(8,128)(2,1)} %copy.49, f32[256,8]{0,1:T(8,128)S(1)} %get-tuple-element.18), kind=kOutput, calls=%fused_computation.8 | convolution fusion | flops 1096810496 | bytes 8658944 | tf_op jit(solution)/shard_map/dot_general | solution.py:83
  71.5 3.9 copy.52
  75.4 6.1 %fusion.27 = f32[4096,512]{1,0:T(8,128)} fusion(bf16[256,4096]{0,1:T(8,128)(2,1)} %bitcast.55, bf16[256,512]{0,1:T(8,128)(2,1)S(1)} %bitcast.63), kind=kOutput, calls=%fused_computation.54 | convolution fusion | flops 1073741824 | bytes 10747904 | tf_op jit(solution)/shard_map/dot_general | solution.py:93
  81.8 3.5 copy.56
  88.7 4.3 multiply_reduce_fusion
  96.1 3.2 convolution_bitcast_fusion
  99.2 2.6 copy.57
  101.8 5.4 copy.58
  107.2 2.6 broadcast_multiply_fusion
  111.8 5.8 %collective-permute-start.3 = (f32[4,512]{1,0:T(4,128)S(1)}, f32[4,512]{1,0:T(4,128)S(1)}, u32[]{:S(2)}, u32[]{:S(2)}) collective-permute-start(f32[4,512]{1,0:T(4,128)S(1)} %bitcast.65), channel_id=1, source_target_pairs={{0,16},{16,32},{32,48},{48,64},{64,80},{80,96},{96,112},{112,128},... | collective-permute-start | bytes 24584 | tf_op jit(solution)/shard_map/ppermute | solution.py:19
  117.6 82.1 %psum.23 = f32[512]{0:T(512)S(1)} all-reduce(f32[512]{0:T(512)S(1)} %get-tuple-element.16), channel_id=1, replica_groups=mesh['seq'=16,'fsdp'=16] {'seq','fsdp'}, use_global_device_ids=true, to_apply=%region_6.0 | all-reduce | flops 512 | bytes 4096 | tf_op jit(solution)/shard_map/psum | solution.py:110
  199.7 9.8 %fusion.10 = f32[8,32,16,16]{2,3,0,1:T(8,128)} fusion(f32[256,32,16,1]{0,2,3,1:T(8,128)} %bitcast.60, bf16[256,8,32,16]{0,3,2,1:T(8,128)(2,1)S(1)} %maximum_multiply_fusion), kind=kOutput, calls=%fused_computation.16 | convolution fusion | flops 201326592 | bytes 2883584 | tf_op jit(solution)/shard_map/pkgc,pgd->kgcd/dot_general | solution.py:107
  214.2 2.7 copy.59
  216.8 2.9 reshape.243
  219.8 2.7 copy.60
  222.4 3.1 concatenate.56
  225.6 3.5 fusion.7
  229.1 234.9 %all-reduce.5.cloned.1.call-done = f32[8,32,16,16]{2,3,0,1:T(8,128)} async-done(((f32[8,32,16,16]{2,3,0,1:T(8,128)}), f32[8,32,16,16]{2,3,0,1:T(8,128)}) %all-reduce.5.cloned.1.call-update) | async-done | bytes 262160 | tf_op jit(solution)/shard_map/psum | solution.py:110
  468.1 95.2 %all-reduce.3.cloned.1.call-done = f32[256,512]{1,0:T(8,128)} async-done(((f32[256,512]{1,0:T(8,128)}), f32[256,512]{1,0:T(8,128)}) %all-reduce.3.cloned.1.call-update) | async-done | bytes 524304 | tf_op jit(solution)/shard_map/psum | solution.py:98
  (81 shorter events, 33.9 us)
Async XLA Ops:
  7.2 56.5 %all-gather.2.cloned.1.call-start = ((), (), s32[]{:S(2)}) async-start(), calls=%async_computation.1 | async-start | bytes 4456448 | tf_op jit(solution)/shard_map/all_gather | solution.py:82
  7.9 217.7 %reduce-scatter.2.cloned.1.call-start = ((), (), s32[]{:S(2)}) async-start(), calls=%async_computation.2 | async-start | bytes 8912896 | tf_op jit(solution)/shard_map/reduce_scatter | solution.py:92
  8.6 30.9 %collective-permute-start.1 = (s32[4]{0:T(128)S(1)}, s32[4]{0:T(128)S(1)}, u32[]{:S(2)}, u32[]{:S(2)}) collective-permute-start(s32[4]{0:T(128)S(1)} %slice_bitcast_fusion.2), channel_id=1, source_target_pairs={{16,0},{32,16},{48,32},{64,48},{80,64},{96,80},{112,96},{128,112},... | collective-permute-start | bytes 56 | tf_op jit(solution)/shard_map/ppermute | solution.py:19
  10.6 29.3 %collective-permute-start = (bf16[4,512]{1,0:T(4,128)(2,1)S(1)}, bf16[4,512]{1,0:T(4,128)(2,1)S(1)}, u32[]{:S(2)}, u32[]{:S(2)}) collective-permute-start(bf16[4,512]{1,0:T(4,128)(2,1)S(1)} %slice_bitcast_fusion.1), channel_id=1, source_target_pairs={{16,0},{32,16},{48,32},{64,48},{80,64},{96,80},{112,96},{128,112},... | collective-permute-start | bytes 12296 | tf_op jit(solution)/shard_map/ppermute | solution.py:19
  12.6 45.6 %collective-permute-start.2 = (bf16[4,512]{1,0:T(4,128)(2,1)S(1)}, bf16[4,512]{1,0:T(4,128)(2,1)S(1)}, u32[]{:S(2)}, u32[]{:S(2)}) collective-permute-start(bf16[4,512]{1,0:T(4,128)(2,1)S(1)} %slice_bitcast_fusion), channel_id=1, source_target_pairs={{16,0},{32,16},{48,32},{64,48},{80,64},{96,80},{112,96},{128,112},... | collective-permute-start | bytes 12296 | tf_op jit(solution)/shard_map/ppermute | solution.py:19
  13.9 9.7 %copy-start.2 = (bf16[1,1024,512]{2,1,0:T(8,128)(2,1)S(1)}, bf16[1,1024,512]{2,1,0:T(8,128)(2,1)}, u32[]{:S(2)}) copy-start(bf16[1,1024,512]{2,1,0:T(8,128)(2,1)} %param.9) | copy-start | bytes 3145732
  23.6 0.8 copy-start.10
  25.2 12.9 %copy-start.11 = (f32[512]{0:T(512)S(1)}, f32[512]{0:T(512)}, u32[]{:S(2)}) copy-start(f32[512]{0:T(512)} %param.12) | copy-start | bytes 6148
  35.0 4.9 copy-start.5
  58.8 1.4 copy-start.6
  58.8 1.9 copy-start.7
  60.7 1.2 copy-start.8
  62.7 0.8 copy-start.4
  81.6 382.5 %all-reduce.5.cloned.1.call-start = ((), (), s32[]{:S(2)}) async-start(), calls=%async_computation.4 | async-start | bytes 4194304 | tf_op jit(solution)/shard_map/psum | solution.py:110
  88.7 4.4 copy-start.9
  109.8 2.0 copy-start
  111.8 113.8 %collective-permute-start.3 = (f32[4,512]{1,0:T(4,128)S(1)}, f32[4,512]{1,0:T(4,128)S(1)}, u32[]{:S(2)}, u32[]{:S(2)}) collective-permute-start(f32[4,512]{1,0:T(4,128)S(1)} %bitcast.65), channel_id=1, source_target_pairs={{0,16},{16,32},{32,48},{48,64},{64,80},{80,96},{96,112},{112,128},... | collective-permute-start | bytes 24584 | tf_op jit(solution)/shard_map/ppermute | solution.py:19
  209.5 353.8 %all-reduce.3.cloned.1.call-start = ((), (), s32[]{:S(2)}) async-start(), calls=%async_computation.3 | async-start | bytes 1048576 | tf_op jit(solution)/shard_map/psum | solution.py:98
  210.4 2.2 copy-start.1
  212.6 1.6 slice-start
  222.4 3.2 copy-start.3
Sparse Core Ops, SparseCore 0:
  9.8 44.4 all-gather.1
  81.7 75.4 reduce-scatter.1
  209.6 254.3 all-reduce.4
  467.1 96.1 all-reduce.2
where the time goes:
time: 574 us; the launch traced here: 572 us
  waiting for transfers between devices  331 us (58%)
  local copies, waits for them, and re-layouts  88.1 us (15%)
  blocking collectives  82.1 us (14%)
  matrix products  32.1 us (6%)
  between operations  15.3 us (3%)
  other arithmetic  13.3 us (2%)
  starting transfers between devices  10.2 us (2%)
    psum x1, waiting for transfers between devices, per_device(): gain_sum, conv_sum = lax.psum((gain_part, conv_part), ('seq', 'fsdp'))  235 us
    psum x1, waiting for transfers between devices, per_device(): proj_sum = lax.psum(panel_part, 'seq')  95.2 us
    psum x1, blocking collectives, per_device(): gain_sum, conv_sum = lax.psum((gain_part, conv_part), ('seq', 'fsdp'))  82.1 us
    concatenate x6, local copies, waits for them, and re-layouts, tap_windows(): return jnp.concatenate([lower, upper], 1)  37.7 us
    unnamed x29, local copies, waits for them, and re-layouts  16.2 us
  transfers between devices with their start and end apart: 8, of which 2 were waited for; matrix products, arithmetic and copies ran while one was open for 18% of the time, Pallas kernels for 0%

commit v1 on v0

--- a/solution.py
+++ b/solution.py
@@ -107,7 +107,7 @@
     conv_part = jnp.einsum(
         "pkgc,pgd->kgcd", grouped_f, grad_hidden, precision=lax.Precision.HIGHEST
     )
-    gain_sum, conv_sum = lax.psum((gain_part, conv_part), ("seq", "fsdp"))
+    gain_sum, conv_sum = lax.psum(lax.psum((gain_part, conv_part), "fsdp"), "seq")
     grad_window = jnp.einsum("pgd,kgcd->pkgc", grad_hidden, conv_f, precision=lax.Precision.HIGHEST)
     grad_window = grad_window.reshape(patches, KERNEL, row_width) * keep_f
     back_lower = grad_window[:, :STRIDE].reshape(length, row_width)

time: 574 us -> 412 us (0.72)
  waiting for transfers between devices: 331 us -> 192 us
  blocking collectives: 82.1 us -> 63.8 us
    psum x1, waiting for transfers between devices: 235 us -> 101 us  [per_device(): lax.psum((gain_part, conv_part), 'fsdp')]
    psum x1, waiting for transfers between devices: 95.2 us -> 18 us  [per_device(): proj_sum = lax.psum(panel_part, 'seq')]
    reduce_scatter x1, waiting for transfers between devices: 0.01 us -> 72.6 us  [per_device(): lax.psum_scatter(lax.dot_general(grad_pre, normed, contract_first, prefer...]
    psum x1 -> x2, blocking collectives: 82.1 us -> 63.8 us  [the longest x1 38.5 us: per_device(): lax.psum(lax.psum((gain_part, conv_part), 'fsdp'), 'seq')]
    unnamed x29 -> x35, local copies, waits for them, and re-layouts: 16.2 us -> 16.1 us
  transfers between devices with their start and end apart: 8 -> 8, of which waited for: 2 -> 3; matrix products, arithmetic and copies ran while one was open for 18% -> 21% of each run, Pallas kernels for 0% -> 0%
where the time goes in v1:
time: 412 us; the launch traced here: 410 us
  waiting for transfers between devices  192 us (47%)
  local copies, waits for them, and re-layouts  88.1 us (21%)
  blocking collectives  63.8 us (15%)
  matrix products  29.9 us (7%)
  between operations  15.3 us (4%)
  other arithmetic  13.2 us (3%)
  starting transfers between devices  7.45 us (2%)
    psum x1, waiting for transfers between devices, per_device(): lax.psum((gain_part, conv_part), 'fsdp')  101 us
    reduce_scatter x1, waiting for transfers between devices, per_device(): lax.psum_scatter(lax.dot_general(grad_pre, normed, contract_first, prefer...  72.6 us
    psum x1, blocking collectives, per_device(): lax.psum(lax.psum((gain_part, conv_part), 'fsdp'), 'seq')  38.5 us
    concatenate x6, local copies, waits for them, and re-layouts, tap_windows(): return jnp.concatenate([lower, upper], 1)  37.7 us
    psum x1, blocking collectives, per_device(): lax.psum((gain_part, conv_part), 'fsdp')  25.2 us
    psum x1, waiting for transfers between devices, per_device(): proj_sum = lax.psum(panel_part, 'seq')  18 us
    unnamed x35, local copies, waits for them, and re-layouts  16.1 us
    dot_general x1, matrix products, per_device(): jnp.einsum('pkgc,pgd->kgcd', grouped_f, grad_hidden, precision=lax.Precis...  9.77 us
  transfers between devices with their start and end apart: 8, of which 3 were waited for; matrix products, arithmetic and copies ran while one was open for 21% of the time, Pallas kernels for 0%

profile of v1, /device:TPU:32, one launch (start us, length us, event | category | flops | bytes accessed | tf_op | source)
XLA Modules:
  0.0 409.6 jit_solution(15400910056296855744)
XLA Ops:
  13.9 9.7 %concatenate.46 = bf16[256,4,32,16]{3,2,1,0:T(8,128)(2,1)} reshape(bf16[1,1024,512]{2,1,0:T(8,128)(2,1)} %param.8) | data formatting | bytes 2097152 | tf_op jit(solution)/shard_map/concatenate | solution.py:48
  25.3 9.8 %copy.43 = bf16[256,4,32,16]{0,3,2,1:T(8,128)(2,1)} copy(bf16[256,4,32,16]{3,2,1,0:T(8,128)(2,1)} %concatenate.46) | data formatting | bytes 2097152 | tf_op jit(solution)/shard_map/concatenate | solution.py:48
  35.1 3.1 copy.65
  40.3 8.2 %concatenate.48 = bf16[256,4,32,16]{3,2,1,0:T(8,128)(2,1)} reshape(bf16[1024,512]{1,0:T(8,128)(2,1)S(1)} %pad_maximum_fusion.1) | data formatting | bytes 2097152 | tf_op jit(solution)/shard_map/concatenate | solution.py:48
  48.5 9.8 %copy.44 = bf16[256,4,32,16]{0,3,2,1:T(8,128)(2,1)} copy(bf16[256,4,32,16]{3,2,1,0:T(8,128)(2,1)} %concatenate.48) | data formatting | bytes 2097152 | tf_op jit(solution)/shard_map/concatenate | solution.py:48
  66.8 7.9 %fusion.6 = bf16[256,8,512]{2,0,1:T(8,128)(2,1)} fusion(bf16[256,512,1]{0,1,2:T(8,128)(2,1)S(1)} %bitcast.62, bf16[8,512,512]{2,1,0:T(8,128)(2,1)} %bitcast.67, bf16[256,4,512]{2,0,1:T(8,128)(2,1)} %copy.50, bf16[256,4,512]{2,0,1:T(8,128)(2,1)} %copy.49, f32[256,8]{0,1:T(8,128)S(1)} %get-tuple-element.20), kind=kOutput, calls=%fused_computation.8 | convolution fusion | flops 1096810496 | bytes 8658944 | tf_op jit(solution)/shard_map/dot_general | solution.py:83
  74.7 3.9 copy.52
  78.6 4.3 %multiply_reduce_fusion = (f32[512]{0:T(512)S(1)}, f32[256]{0:T(256)S(1)}, f32[256,512]{1,0:T(8,128)S(1)}) fusion(f32[256,512]{1,0:T(8,128)} %copy.53, f32[256]{0:T(256)S(1)} %add_rsqrt_fusion, f32[512]{0:T(512)S(1)} %copy-done.14, bf16[256,4096]{0,1:T(8,128)(2,1)} %bitcast.55, bf16[4096,512]{1,0:T(8,128)(2,1)} %all-gather.2.cloned.1.call-done), kind=kOutput, calls=%fused_computation.36 | convolution fusion | flops 1074527488 | bytes 7346176 | tf_op jit(solution)/shard_map/dot_general | solution.py:90
  85.9 9.8 %fusion.10 = f32[8,32,16,16]{2,3,0,1:T(8,128)} fusion(f32[256,32,16,1]{0,2,3,1:T(8,128)} %bitcast.59, bf16[256,8,32,16]{0,3,2,1:T(8,128)(2,1)S(1)} %maximum_multiply_fusion), kind=kOutput, calls=%fused_computation.16 | convolution fusion | flops 201326592 | bytes 2883584 | tf_op jit(solution)/shard_map/pkgc,pgd->kgcd/dot_general | solution.py:107
  97.3 4.5 %fusion.27 = f32[4096,512]{1,0:T(8,128)} fusion(bf16[256,4096]{0,1:T(8,128)(2,1)S(1)} %bitcast.56, bf16[256,512]{0,1:T(8,128)(2,1)S(1)} %bitcast.63), kind=kOutput, calls=%fused_computation.54 | convolution fusion | flops 1073741824 | bytes 10747904 | tf_op jit(solution)/shard_map/dot_general | solution.py:93
  107.8 2.6 copy.57
  110.3 5.4 %copy.58 = f32[256,8,512]{2,0,1:T(8,128)} copy(f32[256,8,512]{0,2,1:T(8,128)} %bitcast.54) | data formatting | bytes 8388608 | tf_op jit(solution)/shard_map/reshape | solution.py:112
  115.7 100.5 %all-reduce.4.cloned.1.call-done = f32[8,32,16,16]{2,3,0,1:T(8,128)} async-done(((f32[8,32,16,16]{2,3,0,1:T(8,128)}), f32[8,32,16,16]{2,3,0,1:T(8,128)}) %all-reduce.4.cloned.1.call-update) | async-done | bytes 262160 | tf_op jit(solution)/shard_map/psum | solution.py:110
  216.2 72.6 %reduce-scatter.2.cloned.1.call-done = f32[256,512]{1,0:T(8,128)} async-done(((f32[4096,512]{1,0:T(8,128)}), f32[256,512]{1,0:T(8,128)}) %reduce-scatter.2.cloned.1.call-update) | async-done | bytes 524304 | tf_op jit(solution)/shard_map/reduce_scatter | solution.py:92
  288.8 2.5 broadcast_multiply_fusion
  293.3 3.5 collective-permute-start.3
  296.8 25.2 %psum.38 = f32[512]{0:T(512)S(1)} all-reduce(f32[512]{0:T(512)S(1)} %get-tuple-element.16), channel_id=1, replica_groups=mesh['seq'=16,'fsdp'=16] {'fsdp'}, use_global_device_ids=true, to_apply=%region_7.0 | all-reduce | flops 512 | bytes 4096 | tf_op jit(solution)/shard_map/psum | solution.py:110
  322.0 38.5 %psum.39 = f32[512]{0:T(512)S(1)} all-reduce(f32[512]{0:T(512)S(1)} %psum.38), channel_id=1, replica_groups=mesh['seq'=16,'fsdp'=16] {'seq'}, use_global_device_ids=true, to_apply=%region_8.0 | all-reduce | flops 512 | bytes 4096 | tf_op jit(solution)/shard_map/psum | solution.py:110
  364.9 2.7 copy.59
  367.6 3.0 reshape.243
  370.6 2.7 copy.60
  373.3 3.1 concatenate.56
  376.4 3.5 fusion.7
  379.9 18.0 %all-reduce.6.cloned.1.call-done = (f32[256,512]{1,0:T(8,128)}, f32[8,32,16,16]{2,3,0,1:T(8,128)}) async-done(((f32[256,512]{1,0:T(8,128)}, f32[8,32,16,16]{2,3,0,1:T(8,128)}), (f32[256,512]{1,0:T(8,128)}, f32[8,32,16,16]{2,3,0,1:T(8,128)})) %all-reduce.6.cloned.1.call-update) | async-done | bytes 786448 | tf_op jit(solution)/shard_map/psum | solution.py:98
  (88 shorter events, 39.5 us)
Async XLA Ops:
  7.2 59.6 %all-gather.2.cloned.1.call-start = ((), (), s32[]{:S(2)}) async-start(), calls=%async_computation.1 | async-start | bytes 4456448 | tf_op jit(solution)/shard_map/all_gather | solution.py:82
  7.9 208.3 %all-reduce.4.cloned.1.call-start = ((), (), s32[]{:S(2)}) async-start(), calls=%async_computation.3 | async-start | bytes 4194304 | tf_op jit(solution)/shard_map/psum | solution.py:110
  8.6 31.0 %collective-permute-start.1 = (s32[4]{0:T(128)S(1)}, s32[4]{0:T(128)S(1)}, u32[]{:S(2)}, u32[]{:S(2)}) collective-permute-start(s32[4]{0:T(128)S(1)} %slice_bitcast_fusion.2), channel_id=1, source_target_pairs={{16,0},{32,16},{48,32},{64,48},{80,64},{96,80},{112,96},{128,112},... | collective-permute-start | bytes 56 | tf_op jit(solution)/shard_map/ppermute | solution.py:19
  10.6 29.4 %collective-permute-start = (bf16[4,512]{1,0:T(4,128)(2,1)S(1)}, bf16[4,512]{1,0:T(4,128)(2,1)S(1)}, u32[]{:S(2)}, u32[]{:S(2)}) collective-permute-start(bf16[4,512]{1,0:T(4,128)(2,1)S(1)} %slice_bitcast_fusion.1), channel_id=1, source_target_pairs={{16,0},{32,16},{48,32},{64,48},{80,64},{96,80},{112,96},{128,112},... | collective-permute-start | bytes 12296 | tf_op jit(solution)/shard_map/ppermute | solution.py:19
  12.6 45.7 %collective-permute-start.2 = (bf16[4,512]{1,0:T(4,128)(2,1)S(1)}, bf16[4,512]{1,0:T(4,128)(2,1)S(1)}, u32[]{:S(2)}, u32[]{:S(2)}) collective-permute-start(bf16[4,512]{1,0:T(4,128)(2,1)S(1)} %slice_bitcast_fusion), channel_id=1, source_target_pairs={{16,0},{32,16},{48,32},{64,48},{80,64},{96,80},{112,96},{128,112},... | collective-permute-start | bytes 12296 | tf_op jit(solution)/shard_map/ppermute | solution.py:19
  13.9 9.7 %copy-start.3 = (bf16[1,1024,512]{2,1,0:T(8,128)(2,1)S(1)}, bf16[1,1024,512]{2,1,0:T(8,128)(2,1)}, u32[]{:S(2)}) copy-start(bf16[1,1024,512]{2,1,0:T(8,128)(2,1)} %param.9) | copy-start | bytes 3145732
  23.6 0.8 copy-start.13
  25.3 12.9 %copy-start.14 = (f32[512]{0:T(512)S(1)}, f32[512]{0:T(512)}, u32[]{:S(2)}) copy-start(f32[512]{0:T(512)} %param.12) | copy-start | bytes 6148
  35.1 4.9 %copy-start.6 = (bf16[1,1024,512]{2,1,0:T(8,128)(2,1)S(1)}, bf16[1,1024,512]{2,1,0:T(8,128)(2,1)}, u32[]{:S(2)}) copy-start(bf16[1,1024,512]{2,1,0:T(8,128)(2,1)} %param.8) | copy-start | bytes 3145732
  58.8 1.4 copy-start.7
  58.8 1.9 copy-start.8
  60.7 1.2 copy-start.9
  78.6 4.4 %copy-start.11 = (f32[256,512]{1,0:T(8,128)S(1)}, f32[256,512]{1,0:T(8,128)}, u32[]{:S(2)}) copy-start(f32[256,512]{1,0:T(8,128)} %copy.53) | copy-start | bytes 1572868
  95.7 1.6 copy-start.2
  95.7 193.1 %reduce-scatter.2.cloned.1.call-start = ((), (), s32[]{:S(2)}) async-start(), calls=%async_computation.2 | async-start | bytes 8912896 | tf_op jit(solution)/shard_map/reduce_scatter | solution.py:92
  101.8 1.0 copy-start.10
  101.8 4.1 %copy-start.5 = (f32[256,512]{0,1:T(8,128)S(1)}, f32[256,512]{0,1:T(8,128)}, u32[]{:S(2)}) copy-start(f32[256,512]{0,1:T(8,128)} %copy.55) | copy-start | bytes 1572868
  101.9 296.0 %all-reduce.6.cloned.1.call-start = ((), (), s32[]{:S(2)}) async-start(), calls=%async_computation.4 | async-start | bytes 5242880 | tf_op jit(solution)/shard_map/psum | solution.py:98
  291.4 1.9 copy-start
  293.3 83.0 %collective-permute-start.3 = (f32[4,512]{1,0:T(4,128)S(1)}, f32[4,512]{1,0:T(4,128)S(1)}, u32[]{:S(2)}, u32[]{:S(2)}) collective-permute-start(f32[4,512]{1,0:T(4,128)S(1)} %bitcast.65), channel_id=1, source_target_pairs={{0,16},{16,32},{32,48},{48,64},{64,80},{80,96},{96,112},{112,128},... | collective-permute-start | bytes 24584 | tf_op jit(solution)/shard_map/ppermute | solution.py:19
  361.1 2.2 copy-start.1
  363.4 1.6 slice-start
  373.3 3.1 copy-start.4
  399.6 2.3 copy-start.12
Sparse Core Ops, SparseCore 0:
  9.8 44.4 all-gather.1
  95.9 120.3 all-reduce.3
  218.8 69.9 reduce-scatter.1
  292.1 105.6 all-reduce.5
